TPU v7x, 128 devices: a whole 4x4x4 slice. The times are simulated.
128 devices in a mesh: req: 8 (over y, core), exp: 16 (over z, x).
Axes of the slice: x: 4, y: 4, z: 4, core: 2. Of those that a mesh axis runs over, the one named last changes fastest.
Arguments:
- hidden: bfloat16 [16384, 2560], P(('req', 'exp')), may hold values from -1.5 to 1.5
- queries: bfloat16 [16384, 1280], P(('req', 'exp')), may hold values from -100 to 100
- suffix_kv: bfloat16 [16384, 512], P(('req', 'exp')), may hold values from -24 to 24
- lengths: int32 [8, 4], P('req'), may hold values from 1 to 1024, 2048 in all within a row
- page_table: int32 [8, 4, 32], P('req'), may hold values from 0 to 55
- page_pool: bfloat16 [56, 128, 512], P('req'), may hold values from -24 to 24
- w_out: bfloat16 [1280, 2560], replicated, may hold values from -0.15625 to 0.15625
- w_router: bfloat16 [2560, 64], replicated, may hold values from -5 to 5
- routes: int32 [16384, 6], P(('req', 'exp')), may hold values from 0 to 63, all different within a row; in each aligned block of 128 rows (0 to 127, 128 to 255, ...) at most 15 rows name the same one
- w_gate: bfloat16 [128, 2560, 768], P(('req', 'exp')), may hold values from -0.125 to 0.125
- w_up: bfloat16 [128, 2560, 768], P(('req', 'exp')), may hold values from -0.125 to 0.125
- w_down: bfloat16 [128, 768, 2560], P(('req', 'exp')), may hold values from -0.4375 to 0.4375
Outputs:
- layer_out: bfloat16 [16384, 2560], P(('req', 'exp'))
Inputs may be any that keep to these rules, and one draw needn't show every extreme that they name: `lengths`: each row sums to 2048; its largest entry is exactly 1024. `page_table`: a page may appear in several prefixes and more than once in one. `routes`: the 6 experts of a token are distinct; among the rows of one device no expert is named more than 15 times, a bound that some block reaches.
All inputs are finite; a program needn't handle non-finite values.
Results may differ from a plain program's by a relative error of at most 0.022.
Values may be sent and summed in bfloat16 or wider, within the bound.
No kernel may reach another device: no remote copies, remote signals or barrier semaphores. Data moves between devices by JAX's collectives and lax.ppermute only.
A program may use at most 192 MiB of HBM per device.

v0:
```python
import math
import jax
import jax.numpy as jnp
from jax import lax
from jax.sharding import PartitionSpec as P

D = 2560
QUERY_HEADS = 10
KEY_VALUE_HEADS = 2
HEAD_SIZE = 128
TOP = 6
PAGE_TOKENS = 128
NEGATIVE_MASK = -1e30
EPS = 1e-06


def fold_scores(carry, query_matrix, key_rows, value_rows, weights):
    scores = jnp.einsum(
        "tgrd,kgd->tgrk", query_matrix, key_rows, preferred_element_type=jnp.float32
    ) * (1.0 / math.sqrt(HEAD_SIZE))
    running_maximum, grand_total, summed_output = carry
    live = weights[:, None, None, :] > 0
    fresh = jnp.maximum(running_maximum, jnp.max(jnp.where(live, scores, NEGATIVE_MASK), axis=-1))
    expo = jnp.where(live, jnp.exp(scores - fresh[..., None]), 0.0) * weights[:, None, None, :]
    decay = jnp.exp(running_maximum - fresh)
    grand_total = decay * grand_total + jnp.sum(expo, axis=-1)
    summed_output = decay[..., None] * summed_output + jnp.einsum(
        "tgrk,kgd->tgrd", expo.astype(jnp.bfloat16), value_rows, preferred_element_type=jnp.float32
    )
    return (fresh, grand_total, summed_output)


def empty_carry(token_count, request_groups):
    return (
        jnp.full((token_count, KEY_VALUE_HEADS, request_groups), NEGATIVE_MASK, jnp.float32),
        jnp.zeros((token_count, KEY_VALUE_HEADS, request_groups), jnp.float32),
        jnp.zeros((token_count, KEY_VALUE_HEADS, request_groups, HEAD_SIZE), jnp.float32),
    )


def on_device(
    hidden,
    queries,
    suffix_kv,
    lengths,
    page_table,
    page_pool,
    w_out,
    w_router,
    routes,
    w_gate,
    w_up,
    w_down,
):
    token_index = hidden.shape[0]
    row_width = KEY_VALUE_HEADS * HEAD_SIZE
    request_groups = QUERY_HEADS // KEY_VALUE_HEADS
    request_count = lax.axis_size("req")
    pool_per_shard = page_pool.shape[0]
    pool_all = pool_per_shard * request_count
    query_matrix = queries.reshape(token_index, KEY_VALUE_HEADS, request_groups, HEAD_SIZE)
    positions = lax.axis_index("exp") * token_index + jnp.arange(token_index, dtype=jnp.int32)
    lens = lengths[0]
    ends = jnp.cumsum(lens)
    starts = ends - lens
    req_of = jnp.sum((positions[:, None] >= ends[None, :]).astype(jnp.int32), axis=1)
    pick = req_of[:, None] == jnp.arange(lens.shape[0], dtype=jnp.int32)[None, :]
    first = jnp.sum(jnp.where(pick, starts[None, :], 0), axis=1)
    counts = jnp.sum(
        (page_table[0][:, :, None] == jnp.arange(pool_all, dtype=jnp.int32)[None, None, :]).astype(
            jnp.float32
        ),
        axis=1,
    )
    query_counts = jnp.dot(pick.astype(jnp.float32), counts, precision=lax.Precision.HIGHEST)
    query_total_set, every_count = (
        lax.all_gather(queries, "req", axis=0, tiled=True),
        lax.all_gather(query_counts.astype(jnp.bfloat16), "req", axis=0, tiled=True),
    )
    query_total_count = query_total_set.shape[0]
    local = lax.dynamic_slice_in_dim(
        every_count, lax.axis_index("req") * pool_per_shard, pool_per_shard, 1
    ).astype(jnp.float32)
    weights = jnp.repeat(local, PAGE_TOKENS, axis=1)
    flattened = page_pool.reshape(pool_per_shard * PAGE_TOKENS, 2 * row_width)
    key_rows = flattened[:, :row_width].reshape(
        pool_per_shard * PAGE_TOKENS, KEY_VALUE_HEADS, HEAD_SIZE
    )
    value_rows = flattened[:, row_width:].reshape(
        pool_per_shard * PAGE_TOKENS, KEY_VALUE_HEADS, HEAD_SIZE
    )
    running_maximum, grand_total, summed_output = fold_scores(
        empty_carry(query_total_count, request_groups),
        query_total_set.reshape(query_total_count, KEY_VALUE_HEADS, request_groups, HEAD_SIZE),
        key_rows,
        value_rows,
        weights,
    )
    peaks, totals, sums = (
        lax.all_to_all(
            running_maximum.reshape(request_count, token_index, KEY_VALUE_HEADS, request_groups),
            "req",
            split_axis=0,
            concat_axis=0,
            tiled=True,
        ),
        lax.all_to_all(
            grand_total.reshape(request_count, token_index, KEY_VALUE_HEADS, request_groups),
            "req",
            split_axis=0,
            concat_axis=0,
            tiled=True,
        ),
        lax.all_to_all(
            summed_output.reshape(
                request_count, token_index, KEY_VALUE_HEADS, request_groups, HEAD_SIZE
            ),
            "req",
            split_axis=0,
            concat_axis=0,
            tiled=True,
        ),
    )
    highest = jnp.max(peaks, axis=0)
    factor = jnp.exp(peaks - highest[None])
    carry = (highest, jnp.sum(factor * totals, axis=0), jnp.sum(factor[..., None] * sums, axis=0))
    segment = lax.all_gather(suffix_kv, "exp", axis=0, tiled=True)
    token_count = segment.shape[0]
    keypos = jnp.arange(token_count, dtype=jnp.int32)
    weights = (
        (keypos[None, :] <= positions[:, None]) & (keypos[None, :] >= first[:, None])
    ).astype(jnp.float32)
    key_rows = segment[:, :row_width].reshape(token_count, KEY_VALUE_HEADS, HEAD_SIZE)
    value_rows = segment[:, row_width:].reshape(token_count, KEY_VALUE_HEADS, HEAD_SIZE)
    running_maximum, grand_total, summed_output = fold_scores(
        carry, query_matrix, key_rows, value_rows, weights
    )
    attended = (
        (summed_output / grand_total[..., None])
        .reshape(token_index, QUERY_HEADS * HEAD_SIZE)
        .astype(jnp.bfloat16)
    )
    projected = jnp.dot(attended, w_out, preferred_element_type=jnp.float32)
    resid = lax.optimization_barrier((hidden.astype(jnp.float32) + projected).astype(jnp.bfloat16))
    resid_f = resid.astype(jnp.float32)
    normed = (resid_f * lax.rsqrt(jnp.mean(resid_f * resid_f, axis=1, keepdims=True) + EPS)).astype(
        jnp.bfloat16
    )
    n_experts = w_router.shape[1]
    logits = jnp.dot(normed, w_router, preferred_element_type=jnp.float32)
    expert_ids = jnp.arange(n_experts, dtype=jnp.int32)
    chosen = jnp.sum(
        jnp.where(routes[:, :, None] == expert_ids[None, None, :], logits[:, None, :], 0.0), axis=2
    )
    gates = jax.nn.softmax(chosen, axis=1)
    capacity = max(2, (5 * token_index * TOP + 4 * n_experts - 1) // (4 * n_experts))
    flat_routes = routes.reshape(-1)
    onehot = (flat_routes[:, None] == expert_ids[None, :]).astype(jnp.int32)
    rank = jnp.sum(jnp.cumsum(onehot, axis=0) * onehot, axis=1) - 1
    slot = flat_routes * capacity + rank
    send = (
        jnp.zeros((n_experts * capacity, D), jnp.bfloat16)
        .at[slot]
        .set(jnp.repeat(normed, TOP, axis=0))
    )
    outgoing = jnp.broadcast_to(
        send.reshape(n_experts, 1, capacity, D), (n_experts, 2, capacity, D)
    ).reshape(2 * n_experts, capacity, D)
    rows = lax.all_to_all(outgoing, ("req", "exp"), split_axis=0, concat_axis=0, tiled=True)
    array_shape = rows.shape
    flat_rows = rows.reshape(-1, D)
    gate_part = jnp.dot(flat_rows, w_gate[0], preferred_element_type=jnp.float32)
    up_part = jnp.dot(flat_rows, w_up[0], preferred_element_type=jnp.float32)
    inner = (jax.nn.silu(gate_part) * up_part).astype(jnp.bfloat16)
    returned = lax.all_to_all(
        jnp.dot(inner, w_down[0], preferred_element_type=jnp.float32)
        .astype(jnp.bfloat16)
        .reshape(array_shape),
        ("req", "exp"),
        split_axis=0,
        concat_axis=0,
        tiled=True,
    )
    halves = jnp.sum(
        returned.reshape(n_experts, 2, capacity, D).astype(jnp.float32), axis=1
    ).reshape(n_experts * capacity, D)
    picked = halves[slot].reshape(token_index, TOP, D)
    moe = jnp.sum(picked * gates[:, :, None], axis=1)
    return (resid_f + moe).astype(jnp.bfloat16)


def solution(mesh):
    placed = (
        P(("req", "exp"), None),
        P(("req", "exp"), None),
        P(("req", "exp"), None),
        P("req", None),
        P("req", None, None),
        P("req", None, None),
        P(),
        P(),
        P(("req", "exp"), None),
        P(("req", "exp"), None, None),
        P(("req", "exp"), None, None),
        P(("req", "exp"), None, None),
    )
    return jax.shard_map(
        on_device, mesh=mesh, in_specs=placed, out_specs=P(("req", "exp"), None), check_vma=False
    )
```

profile of v0, /device:TPU:34, one launch (start us, length us, event | category | flops | bytes accessed | tf_op | source)
XLA Modules:
  0.0 631.7 jit_solution(13155531788352508001)
XLA Ops:
  7.4 1.9 copy.159
  9.3 0.8 reduce-window.10
  10.2 0.8 convert_reduce_fusion.1
  11.2 12.1 %all_gather.9 = bf16[1024,56]{0,1:T(8,128)(2,1)S(1)} all-gather(bf16[128,56]{0,1:T(8,128)(2,1)S(1)} %convolution_convert_fusion.1), channel_id=1, replica_groups=mesh['req'=8,'exp'=16] {'req'}, dimensions={0}, use_global_device_ids=true | all-gather | bytes 129024 | tf_op jit(solution)/shard_map/all_gather | solution.py:78
  23.6 1.2 fusion.66
  25.1 16.3 %all-gather.3.cloned.1.call-done = bf16[1024,1280]{0,1:T(8,128)(2,1)} async-done(((bf16[128,1280]{0,1:T(8,128)(2,1)}), bf16[1024,1280]{0,1:T(8,128)(2,1)}) %all-gather.3.cloned.1.call-update) | async-done | bytes 2621456 | tf_op jit(solution)/shard_map/all_gather | solution.py:77
  41.4 16.3 %fusion = (f32[1024,2,5]{0,2,1:T(8,128)S(1)}, f32[2,896,1024,5]{2,1,3,0:T(8,128)}) fusion(pred[1024,896]{0,1:T(8,128)(4,1)S(1)} %bitcast_compare_fusion, bf16[896,2,128,1]{0,2,3,1:T(8,128)(2,1)S(1)} %bitcast.144, bf16[1024,2,5,128]{0,3,2,1:T(8,128)(2,1)} %bitcast.140), kind=kOutput, calls=%fused_computation.4 | convolution fusion | flops 2376325120 | bytes 40738816 | tf_op jit(solution)/shard_map/tgrd,kgd->tgrk/dot_general | solution.py:18
  57.7 0.4 broadcast_in_dim.118
  58.2 1.8 copy-done.1
  60.0 15.7 %fusion.4 = f32[1024,2,5]{0,2,1:T(8,128)S(1)} fusion(f32[2,896,1024,5]{2,1,3,0:T(8,128)} %get-tuple-element.18, f32[1024,896]{0,1:T(8,128)S(1)} %bitcast.138, f32[1024,2,5]{0,2,1:T(8,128)S(1)} %get-tuple-element.14, pred[1024,896]{0,1:T(8,128)(4,1)S(1)} %bitcast_compare_fusion), kind=kLoop, calls=%fused_computation.8 | loop fusion | flops 45864960 | bytes 41369600 | tf_op jit(solution)/shard_map/reduce_sum | solution.py:26
  75.7 0.6 copy.183
  76.3 4.0 all-to-all-start.2
  80.4 0.8 copy.165
  81.4 0.6 copy.163
  82.1 3.8 all-to-all-done.2
  85.8 3.3 all-to-all-start
  89.2 17.4 %bitcast_add_fusion = f32[1024,2,5,128]{3,0,2,1:T(8,128)S(1)} fusion(f32[1024,2,5]{0,2,1:T(8,128)S(1)} %get-tuple-element.13, bf16[896,2,128,1]{0,2,3,1:T(8,128)(2,1)S(1)} %bitcast.148, f32[2,896,1024,5]{2,1,3,0:T(8,128)} %get-tuple-element.18, f32[1024,896]{0,1:T(8,128)} %bitcast.139, f32[1024,2,5]{0,2,1:T(8,128)S(1)} %get-tuple-element.14, ...), kind=kOutput, calls=%fused_computation.24 | convolution fusion | flops 2395996160 | bytes 47071232 | tf_op jit(solution)/shard_map/tgrk,kgd->tgrd/dot_general | solution.py:27
  106.6 2.7 copy.177
  109.4 5.1 all-to-all-start.1
  114.9 1.8 reduce-window.11
  117.9 12.6 %all-gather.5.cloned.1.call-done = bf16[2048,512]{0,1:T(8,128)(2,1)} async-done(((bf16[128,512]{0,1:T(8,128)(2,1)}), bf16[2048,512]{0,1:T(8,128)(2,1)}) %all-gather.5.cloned.1.call-update) | async-done | bytes 2097168 | tf_op jit(solution)/shard_map/all_gather | solution.py:127
  130.5 2.7 fusion.65
  133.2 5.8 fusion.9
  139.2 6.4 %fusion.13 = f32[128,2,5]{0,2,1:T(8,128)S(1)} fusion(f32[2,2048,128,5]{2,1,3,0:T(8,128)} %get-tuple-element.20, f32[128,2048]{0,1:T(8,128)S(1)} %get-tuple-element.16, f32[128,2,5]{0,2,1:T(8,128)S(1)} %copy.180, pred[128,2048]{0,1:T(8,128)(4,1)S(1)} %get-tuple-element.15), kind=kLoop, calls=%fused_computation.21 | loop fusion | flops 13105920 | bytes 11806720 | tf_op jit(solution)/shard_map/reduce_sum | solution.py:26
  145.7 29.8 %all-to-all-done.1 = f32[8,128,2,5,128]{4,1,3,2,0:T(8,128)} async-done(((f32[8,128,2,5,128]{4,1,3,2,0:T(8,128)}), f32[8,128,2,5,128]{4,1,3,2,0:T(8,128)}, u32[]{:S(2)}, u32[]{:S(2)}) %all-to-all-start.1) | async-done | bytes 5242912 | tf_op jit(solution)/shard_map/all_to_all | solution.py:114
  175.4 4.3 multiply_reduce_fusion.1
  179.8 2.2 copy.179
  181.9 7.9 %fusion.43 = bf16[128,2,5,128]{0,3,2,1:T(8,128)(2,1)S(1)} fusion(bf16[2048,2,128,1]{0,2,3,1:T(8,128)(2,1)} %bitcast.146, f32[2,2048,128,5]{2,1,3,0:T(8,128)} %get-tuple-element.20, f32[128,2048]{0,1:T(8,128)} %copy-done.3, f32[128,2,5]{0,2,1:T(8,128)S(1)} %copy.180, pred[128,2048]{0,1:T(8,128)(4,1)S(1)} %get-tuple-element.15, ...), kind=kOutput, calls=%fused_computation.52 | convolution fusion | flops 684851200 | bytes 13843456 | tf_op jit(solution)/shard_map/tgrk,kgd->tgrd/dot_general | solution.py:27
  189.8 1.1 fusion.23
  191.3 2.9 broadcast_in_dim.133
  194.2 7.5 %reshape.302 = bf16[768,2560]{1,0:T(8,128)(2,1)} reshape(bf16[128,6,2560]{2,1,0:T(8,128)(2,1)} %broadcast_in_dim.133) | data formatting | bytes 7864320 | tf_op jit(solution)/shard_map/reshape | solution.py:164
  201.7 12.2 %scatter_custom_fusion = bf16[960,2560]{1,0:T(8,128)(2,1)} fusion(s32[768]{0:T(1024)S(1)} %fusion.56, bf16[768,2560]{1,0:T(8,128)(2,1)} %reshape.302, bf16[]{:T(256)} %constant.29.clone.1), kind=kCustom, calls=%fused_computation.35 | custom fusion | bytes 4915712 | tf_op jit(solution)/shard_map/scatter | solution.py:164
  213.9 7.6 %broadcast_in_dim.134 = bf16[64,15,2560]{2,1,0:T(8,128)(2,1)} reshape(bf16[960,2560]{1,0:T(8,128)(2,1)} %scatter_custom_fusion) | data formatting | bytes 9830400 | tf_op jit(solution)/shard_map/broadcast_in_dim | solution.py:166
  221.4 7.8 %broadcast_in_dim.135 = bf16[64,2,15,2560]{3,2,1,0:T(8,128)(2,1)} broadcast(bf16[64,15,2560]{2,1,0:T(8,128)(2,1)} %broadcast_in_dim.134), dimensions={0,2,3} | broadcast | bytes 14745600 | tf_op jit(solution)/shard_map/broadcast_in_dim | solution.py:166
  229.2 127.0 %all_to_all.25 = bf16[128,15,2560]{2,1,0:T(8,128)(2,1)} all-to-all(bf16[128,15,2560]{2,1,0:T(8,128)(2,1)} %bitcast.135), channel_id=1, replica_groups=mesh['req'=8,'exp'=16] {'req','exp'}, dimensions={0} | all-to-all | bytes 19660800 | tf_op jit(solution)/shard_map/all_to_all | solution.py:169
  356.2 13.9 %reshape.285 = bf16[1920,2560]{1,0:T(8,128)(2,1)} reshape(bf16[128,15,2560]{2,1,0:T(8,128)(2,1)} %all_to_all.25) | data formatting | bytes 19660800 | tf_op jit(solution)/shard_map/reshape | solution.py:171
  370.1 13.1 %fusion.21 = f32[1920,768]{1,0:T(8,128)} fusion(bf16[1920,2560]{1,0:T(8,128)(2,1)} %reshape.285, bf16[1,2560,768]{2,1,0:T(8,128)(2,1)} %param.21), kind=kOutput, calls=%fused_computation.30 | convolution fusion | flops 7549747200 | bytes 19660800 | tf_op jit(solution)/shard_map/dot_general | solution.py:172
  383.2 27.3 %convolution_convert_fusion = bf16[1920,2560]{1,0:T(8,128)(2,1)} fusion(f32[1920,768]{1,0:T(8,128)} %fusion.21, bf16[1920,2560]{1,0:T(8,128)(2,1)} %reshape.285, bf16[1,768,2560]{2,1,0:T(8,128)(2,1)} %param.23, bf16[1,2560,768]{2,1,0:T(8,128)(2,1)} %param.22), kind=kOutput, calls=%fused_computation.13 | convolution fusion | flops 15113256960 | bytes 33423360 | tf_op jit(solution)/shard_map/dot_general | solution.py:176
  410.5 13.8 %reshape.286 = bf16[128,15,2560]{2,1,0:T(8,128)(2,1)} reshape(bf16[1920,2560]{1,0:T(8,128)(2,1)} %convolution_convert_fusion) | data formatting | bytes 19660800 | tf_op jit(solution)/shard_map/reshape | solution.py:178
  424.3 7.0 %all-to-all-start.4 = ((bf16[128,15,2560]{2,1,0:T(8,128)(2,1)}), bf16[128,15,2560]{2,1,0:T(8,128)(2,1)}, u32[]{:S(2)}, u32[]{:S(2)}) async-start(bf16[128,15,2560]{2,1,0:T(8,128)(2,1)} %reshape.286), calls=%async_computation.4 | async-start | bytes 20971520 | tf_op jit(solution)/shard_map/all_to_all | solution.py:175
  431.3 0.3 fusion.67
  431.9 140.3 %all-to-all-done.4 = bf16[128,15,2560]{2,1,0:T(8,128)(2,1)} async-done(((bf16[128,15,2560]{2,1,0:T(8,128)(2,1)}), bf16[128,15,2560]{2,1,0:T(8,128)(2,1)}, u32[]{:S(2)}, u32[]{:S(2)}) %all-to-all-start.4) | async-done | bytes 9830432 | tf_op jit(solution)/shard_map/all_to_all | solution.py:175
  572.1 11.3 %convert_reduce_fusion = f32[64,15,2560]{2,1,0:T(8,128)} fusion(bf16[128,15,2560]{2,1,0:T(8,128)(2,1)} %all-to-all-done.4), kind=kLoop, calls=%fused_computation.10 | loop fusion | flops 7372800 | bytes 19660800 | tf_op jit(solution)/shard_map/reduce_sum | solution.py:184
  583.5 10.2 %reshape.287 = f32[960,2560]{1,0:T(8,128)} reshape(f32[64,15,2560]{2,1,0:T(8,128)} %convert_reduce_fusion) | data formatting | bytes 19660800 | tf_op jit(solution)/shard_map/reshape | solution.py:186
  593.7 12.2 %gather_fusion = f32[768,2560]{1,0:T(8,128)} fusion(f32[960,2560]{1,0:T(8,128)} %reshape.287, s32[1024]{0:T(1024)S(1)} %pad_clamp_fusion), kind=kCustom, calls=%fused_computation | custom fusion | bytes 15731712 | tf_op jit(solution)/shard_map/gather | solution.py:187
  605.9 9.2 %reshape.288 = f32[128,6,2560]{2,1,0:T(8,128)} reshape(f32[768,2560]{1,0:T(8,128)} %gather_fusion) | data formatting | bytes 15728640 | tf_op jit(solution)/shard_map/reshape | solution.py:187
  615.2 7.9 %multiply_reduce_fusion = f32[128,2560]{1,0:T(8,128)S(1)} fusion(f32[128,6,2560]{2,1,0:T(8,128)} %reshape.288, f32[128,6]{1,0:T(8,128)S(1)} %copy.192), kind=kLoop, calls=%fused_computation.20 | loop fusion | flops 3604480 | bytes 9178112 | tf_op jit(solution)/shard_map/reduce_sum | solution.py:188
  623.1 0.9 fusion.31
  (69 shorter events, 3.5 us)
Async XLA Ops:
  7.4 424.0 %copy-start = (bf16[2560,64]{0,1:T(8,128)(2,1)S(1)}, bf16[2560,64]{0,1:T(8,128)(2,1)}, u32[]{:S(2)}) copy-start(bf16[2560,64]{0,1:T(8,128)(2,1)} %param.19) | copy-start | bytes 983044
  7.4 34.0 %all-gather.3.cloned.1.call-start = ((), (), s32[]{:S(2)}) async-start(), calls=%async_computation.5 | async-start | bytes 2949120 | tf_op jit(solution)/shard_map/all_gather | solution.py:77
  58.2 1.8 copy-start.1
  60.0 20.4 %copy-start.5 = (bf16[128,512]{1,0:T(8,128)(2,1)S(1)}, bf16[128,512]{1,0:T(8,128)(2,1)}, u32[]{:S(2)}) copy-start(bf16[128,512]{1,0:T(8,128)(2,1)} %param.14) | copy-start | bytes 393220
  76.3 9.5 %all-to-all-start.2 = ((f32[8,128,2,5]{1,2,3,0:T(2,128)}), f32[8,128,2,5]{1,2,3,0:T(2,128)S(1)}, u32[]{:S(2)}, u32[]{:S(2)}) async-start(f32[8,128,2,5]{1,2,3,0:T(2,128)} %copy.183), calls=%async_computation.2 | async-start | bytes 81920 | tf_op jit(solution)/shard_map/all_to_all | solution.py:107
  80.3 50.2 %all-gather.5.cloned.1.call-start = ((), (), s32[]{:S(2)}) async-start(), calls=%async_computation.6 | async-start | bytes 2228224 | tf_op jit(solution)/shard_map/all_gather | solution.py:127
  85.8 23.5 %all-to-all-start = ((f32[8,128,2,5]{1,2,3,0:T(2,128)}), f32[8,128,2,5]{1,2,3,0:T(2,128)S(1)}, u32[]{:S(2)}, u32[]{:S(2)}) async-start(f32[8,128,2,5]{1,2,3,0:T(2,128)} %copy.163), calls=%async_computation | async-start | bytes 81920 | tf_op jit(solution)/shard_map/all_to_all | solution.py:100
  109.3 5.1 copy-start.6
  109.4 8.1 %copy-start.7 = (s32[1,4]{1,0:T(1,128)S(1)}, s32[1,4]{1,0:T(1,128)}, u32[]{:S(2)}) copy-start(s32[1,4]{1,0:T(1,128)} %param.15) | copy-start | bytes 52
  109.4 23.9 %copy-start.2 = (bf16[128,1280]{0,1:T(8,128)(2,1)S(1)}, bf16[128,1280]{0,1:T(8,128)(2,1)}, u32[]{:S(2)}) copy-start(bf16[128,1280]{0,1:T(8,128)(2,1)} %copy.159) | copy-start | bytes 983044
  109.4 66.1 %all-to-all-start.1 = ((f32[8,128,2,5,128]{4,1,3,2,0:T(8,128)}), f32[8,128,2,5,128]{4,1,3,2,0:T(8,128)}, u32[]{:S(2)}, u32[]{:S(2)}) async-start(f32[8,128,2,5,128]{4,1,3,2,0:T(8,128)} %copy.177), calls=%async_computation.1 | async-start | bytes 10485760 | tf_op jit(solution)/shard_map/all_to_all | solution.py:114
  117.9 21.3 %copy-start.3 = (f32[128,2048]{0,1:T(8,128)}, f32[128,2048]{0,1:T(8,128)S(1)}, u32[]{:S(2)}) copy-start(f32[128,2048]{0,1:T(8,128)S(1)} %get-tuple-element.16) | copy-start | bytes 3145732
  175.4 14.4 %slice-start = ((s8[6553600]{0:T(1024)(128)(4,1)}), s8[2359296]{0:T(1024)(128)(4,1)S(1)}, s32[]{:S(2)}) async-start(s8[6553600]{0:T(1024)(128)(4,1)} %bitcast.136), calls=%async_computation.7 | async-start | bytes 4718592
  181.9 7.9 %slice-start.1 = ((s8[6553600]{0:T(1024)(128)(4,1)}), s8[4194304]{0:T(1024)(128)(4,1)S(1)}, s32[]{:S(2)}) async-start(s8[6553600]{0:T(1024)(128)(4,1)} %bitcast.136), calls=%async_computation.8 | async-start | bytes 8388608
  181.9 7.9 %copy-start.4 = (bf16[128,2560]{1,0:T(8,128)(2,1)S(1)}, bf16[128,2560]{1,0:T(8,128)(2,1)}, u32[]{:S(2)}) copy-start(bf16[128,2560]{1,0:T(8,128)(2,1)} %param.12) | copy-start | bytes 1966084
  424.3 147.8 %all-to-all-start.4 = ((bf16[128,15,2560]{2,1,0:T(8,128)(2,1)}), bf16[128,15,2560]{2,1,0:T(8,128)(2,1)}, u32[]{:S(2)}, u32[]{:S(2)}) async-start(bf16[128,15,2560]{2,1,0:T(8,128)(2,1)} %reshape.286), calls=%async_computation.4 | async-start | bytes 20971520 | tf_op jit(solution)/shard_map/all_to_all | solution.py:175
Sparse Core Ops, SparseCore 0:
  9.9 31.4 all-gather.2
Sparse Core Ops, SparseCore 1:
  82.9 47.5 all-gather.4
where the time goes:
time: 642 us; the launch traced here: 632 us
  waiting for transfers between devices  203 us (32%)
  blocking collectives  139 us (22%)
  local copies, waits for them, and re-layouts  114 us (18%)
  matrix products  89.5 us (14%)
  other arithmetic  51.6 us (8%)
  starting transfers between devices  19.5 us (3%)
  between operations  15.4 us (2%)
    all_to_all x1, waiting for transfers between devices, on_device(): lax.all_to_all(jnp.dot(inner, w_down[0], preferred_element_type=jnp.float...  140 us
    all_to_all x1, blocking collectives, on_device(): lax.all_to_all(outgoing, ('req', 'exp'), split_axis=0, concat_axis=0, til...  127 us
    all_to_all x1, waiting for transfers between devices, on_device(): lax.all_to_all(summed_output.reshape(request_count, token_index, KEY_VALU...  29.8 us
    dot_general x1, matrix products, on_device(): jnp.dot(inner, w_down[0], preferred_element_type=jnp.float32)  27.3 us
    dot_general x2, matrix products, fold_scores(): jnp.einsum('tgrk,kgd->tgrd', expo.astype(jnp.bfloat16), value_rows, prefe...  25.3 us
    dot_general x2, matrix products, fold_scores(): jnp.einsum('tgrd,kgd->tgrk', query_matrix, key_rows, preferred_element_ty...  22.1 us
    reduce_sum x2, other arithmetic, fold_scores(): grand_total = decay * grand_total + jnp.sum(expo, axis=-1)  22.1 us
    all_gather x1, waiting for transfers between devices, on_device(): lax.all_gather(queries, 'req', axis=0, tiled=True)  16.3 us
  transfers between devices with their start and end apart: 6, of which 5 were waited for; matrix products, arithmetic and copies ran while one was open for 7% of the time, Pallas kernels for 0%

commit v1 on v0

--- a/solution.py
+++ b/solution.py
@@ -74,7 +74,12 @@
     )
     query_counts = jnp.dot(pick.astype(jnp.float32), counts, precision=lax.Precision.HIGHEST)
     query_total_set, every_count = (
-        lax.all_gather(queries, "req", axis=0, tiled=True),
+        jnp.concatenate(
+            lax.all_to_all(
+                jnp.stack([queries for _ in range(lax.axis_size("req"))], axis=0), "req", 0, 0
+            ),
+            axis=0,
+        ),
         lax.all_gather(query_counts.astype(jnp.bfloat16), "req", axis=0, tiled=True),
     )
     query_total_count = query_total_set.shape[0]

time: 642 us -> 667 us (1.039)
  blocking collectives: 139 us -> 165 us
  local copies, waits for them, and re-layouts: 114 us -> 132 us
  waiting for transfers between devices: 203 us -> 190 us
    all_gather x1, blocking collectives: 12.1 us -> 37.5 us  [on_device(): lax.all_gather(query_counts.astype(jnp.bfloat16), 'req', axis=0, tiled=True)]
    all_gather x1 -> x0, waiting for transfers between devices: 16.3 us -> none  [on_device(): lax.all_gather(queries, 'req', axis=0, tiled=True)]
    all_to_all x0 -> x1, local copies, waits for them, and re-layouts: none -> 9.19 us  [on_device(): lax.all_to_all(jnp.stack([queries for _ in range(lax.axis_size('req'))],...]
    another operation x0 -> x2, local copies, waits for them, and re-layouts: none -> 7.05 us  [the longest x1 5.18 us: on_device(): query_total_set.reshape(query_total_count, KEY_VALUE_HEADS, request_group...]
  transfers between devices with their start and end apart: 6 -> 6, of which waited for: 5 -> 4; matrix products, arithmetic and copies ran while one was open for 7% -> 5% of each run, Pallas kernels for 0% -> 0%
where the time goes in v1:
time: 667 us; the launch traced here: 657 us
  waiting for transfers between devices  190 us (28%)
  blocking collectives  165 us (25%)
  local copies, waits for them, and re-layouts  132 us (20%)
  matrix products  85.6 us (13%)
  other arithmetic  46.3 us (7%)
  starting transfers between devices  23.1 us (3%)
  between operations  14 us (2%)
    all_to_all x1, waiting for transfers between devices, on_device(): lax.all_to_all(jnp.dot(inner, w_down[0], preferred_element_type=jnp.float...  140 us
    all_to_all x1, blocking collectives, on_device(): lax.all_to_all(outgoing, ('req', 'exp'), split_axis=0, concat_axis=0, til...  128 us
    all_gather x1, blocking collectives, on_device(): lax.all_gather(query_counts.astype(jnp.bfloat16), 'req', axis=0, tiled=True)  37.5 us
    all_to_all x1, waiting for transfers between devices, on_device(): lax.all_to_all(summed_output.reshape(request_count, token_index, KEY_VALU...  32.4 us
    dot_general x1, matrix products, on_device(): jnp.dot(inner, w_down[0], preferred_element_type=jnp.float32)  27.3 us
    dot_general x2, matrix products, fold_scores(): jnp.einsum('tgrk,kgd->tgrd', expo.astype(jnp.bfloat16), value_rows, prefe...  25.3 us
    dot_general x2, matrix products, fold_scores(): jnp.einsum('tgrd,kgd->tgrk', query_matrix, key_rows, preferred_element_ty...  18.2 us
    reduce_sum x2, other arithmetic, fold_scores(): grand_total = decay * grand_total + jnp.sum(expo, axis=-1)  18.1 us
  transfers between devices with their start and end apart: 6, of which 4 were waited for; matrix products, arithmetic and copies ran while one was open for 5% of the time, Pallas kernels for 0%

profile of v1, /device:TPU:34, one launch (start us, length us, event | category | flops | bytes accessed | tf_op | source)
XLA Modules:
  0.0 656.7 jit_solution(15504776445954894416)
XLA Ops:
  6.5 1.3 copy.162
  7.8 1.9 stack.2
  9.7 4.5 all-to-all-start
  14.8 37.5 %all_gather.6 = bf16[1024,56]{0,1:T(8,128)(2,1)S(1)} all-gather(bf16[128,56]{0,1:T(8,128)(2,1)S(1)} %convolution_convert_fusion.1), channel_id=1, replica_groups=mesh['req'=8,'exp'=16] {'req'}, dimensions={0}, use_global_device_ids=true | all-gather | bytes 129024 | tf_op jit(solution)/shard_map/all_gather | solution.py:83
  52.8 9.2 %copy.163 = bf16[8,128,1280]{1,0,2:T(8,128)(2,1)} copy(bf16[8,128,1280]{1,2,0:T(8,128)(2,1)} %all-to-all-done) | data formatting | bytes 5242880 | tf_op jit(solution)/shard_map/all_to_all | solution.py:78
  62.0 5.2 reshape_reshape.3
  67.2 16.3 %fusion = (f32[1024,2,5]{0,2,1:T(8,128)S(1)}, f32[2,896,1024,5]{2,1,3,0:T(8,128)}) fusion(pred[1024,896]{0,1:T(8,128)(4,1)S(1)} %bitcast_compare_fusion, bf16[896,2,128,1]{0,2,3,1:T(8,128)(2,1)S(1)} %bitcast.144, bf16[1024,2,5,128]{0,3,2,1:T(8,128)(2,1)} %reshape_reshape.3), kind=kOutput, calls=%fused_computation.4 | convolution fusion | flops 2376325120 | bytes 40738816 | tf_op jit(solution)/shard_map/tgrd,kgd->tgrk/dot_general | solution.py:18
  83.6 0.4 broadcast_in_dim.118
  84.0 1.8 copy-done.2
  85.8 15.7 %fusion.4 = f32[1024,2,5]{0,2,1:T(8,128)S(1)} fusion(f32[2,896,1024,5]{2,1,3,0:T(8,128)} %get-tuple-element.18, f32[1024,896]{0,1:T(8,128)S(1)} %bitcast.139, f32[1024,2,5]{0,2,1:T(8,128)S(1)} %get-tuple-element.14, pred[1024,896]{0,1:T(8,128)(4,1)S(1)} %bitcast_compare_fusion), kind=kLoop, calls=%fused_computation.8 | loop fusion | flops 45864960 | bytes 41369600 | tf_op jit(solution)/shard_map/reduce_sum | solution.py:26
  101.5 0.6 copy.187
  102.2 3.3 all-to-all-start.3
  105.6 0.8 copy.169
  106.6 0.6 copy.167
  107.3 3.7 all-to-all-done.3
  110.9 3.5 all-to-all-start.1
  114.5 17.5 %bitcast_add_fusion = f32[1024,2,5,128]{3,0,2,1:T(8,128)S(1)} fusion(f32[1024,2,5]{0,2,1:T(8,128)S(1)} %get-tuple-element.13, bf16[896,2,128,1]{0,2,3,1:T(8,128)(2,1)S(1)} %bitcast.148, f32[2,896,1024,5]{2,1,3,0:T(8,128)} %get-tuple-element.18, f32[1024,896]{0,1:T(8,128)} %bitcast.140, f32[1024,2,5]{0,2,1:T(8,128)S(1)} %get-tuple-element.14, ...), kind=kOutput, calls=%fused_computation.24 | convolution fusion | flops 2395996160 | bytes 47071232 | tf_op jit(solution)/shard_map/tgrk,kgd->tgrd/dot_general | solution.py:27
  132.0 2.7 copy.181
  134.7 4.7 all-to-all-start.2
  139.8 1.8 reduce-window.11
  142.9 14.0 %all-gather.2.cloned.1.call-done = bf16[2048,512]{0,1:T(8,128)(2,1)} async-done(((bf16[128,512]{0,1:T(8,128)(2,1)}), bf16[2048,512]{0,1:T(8,128)(2,1)}) %all-gather.2.cloned.1.call-update) | async-done | bytes 2097168 | tf_op jit(solution)/shard_map/all_gather | solution.py:132
  156.9 2.7 fusion.65
  159.6 1.9 fusion.9
  161.5 3.9 copy-done.1
  165.5 2.4 fusion.13
  168.0 32.4 %all-to-all-done.2 = f32[8,128,2,5,128]{4,1,3,2,0:T(8,128)} async-done(((f32[8,128,2,5,128]{4,1,3,2,0:T(8,128)}), f32[8,128,2,5,128]{4,1,3,2,0:T(8,128)}, u32[]{:S(2)}, u32[]{:S(2)}) %all-to-all-start.2) | async-done | bytes 5242912 | tf_op jit(solution)/shard_map/all_to_all | solution.py:119
  200.4 4.3 multiply_reduce_fusion.1
  204.7 2.2 copy.183
  206.9 7.9 %fusion.43 = bf16[128,2,5,128]{0,3,2,1:T(8,128)(2,1)S(1)} fusion(bf16[2048,2,128,1]{0,2,3,1:T(8,128)(2,1)} %bitcast.146, f32[2,2048,128,5]{2,1,3,0:T(8,128)} %copy-done.1, f32[128,2048]{0,1:T(8,128)} %copy-done.3, f32[128,2,5]{0,2,1:T(8,128)S(1)} %copy.184, pred[128,2048]{0,1:T(8,128)(4,1)S(1)} %get-tuple-element.15, f32[128,2,5,128]{0,3,2,1:T(8,128)} %copy.183, ...), kind=kOutput, calls=%fused_computation.52 | convolution fusion | flops 684851200 | bytes 13843456 | tf_op jit(solution)/shard_map/tgrk,kgd->tgrd/dot_general | solution.py:27
  214.8 1.0 fusion.23
  216.3 2.9 broadcast_in_dim.133
  219.2 7.5 %reshape.300 = bf16[768,2560]{1,0:T(8,128)(2,1)} reshape(bf16[128,6,2560]{2,1,0:T(8,128)(2,1)} %broadcast_in_dim.133) | data formatting | bytes 7864320 | tf_op jit(solution)/shard_map/reshape | solution.py:169
  226.7 12.2 %scatter_custom_fusion = bf16[960,2560]{1,0:T(8,128)(2,1)} fusion(s32[768]{0:T(1024)S(1)} %fusion.56, bf16[768,2560]{1,0:T(8,128)(2,1)} %reshape.300, bf16[]{:T(256)} %constant.29.clone.1), kind=kCustom, calls=%fused_computation.35 | custom fusion | bytes 4915712 | tf_op jit(solution)/shard_map/scatter | solution.py:169
  238.9 7.6 %broadcast_in_dim.134 = bf16[64,15,2560]{2,1,0:T(8,128)(2,1)} reshape(bf16[960,2560]{1,0:T(8,128)(2,1)} %scatter_custom_fusion) | data formatting | bytes 9830400 | tf_op jit(solution)/shard_map/broadcast_in_dim | solution.py:171
  246.4 7.8 %broadcast_in_dim.135 = bf16[64,2,15,2560]{3,2,1,0:T(8,128)(2,1)} broadcast(bf16[64,15,2560]{2,1,0:T(8,128)(2,1)} %broadcast_in_dim.134), dimensions={0,2,3} | broadcast | bytes 14745600 | tf_op jit(solution)/shard_map/broadcast_in_dim | solution.py:171
  254.2 127.5 %all_to_all.30 = bf16[128,15,2560]{2,1,0:T(8,128)(2,1)} all-to-all(bf16[128,15,2560]{2,1,0:T(8,128)(2,1)} %bitcast.136), channel_id=1, replica_groups=mesh['req'=8,'exp'=16] {'req','exp'}, dimensions={0} | all-to-all | bytes 19660800 | tf_op jit(solution)/shard_map/all_to_all | solution.py:174
  381.8 13.9 %reshape.283 = bf16[1920,2560]{1,0:T(8,128)(2,1)} reshape(bf16[128,15,2560]{2,1,0:T(8,128)(2,1)} %all_to_all.30) | data formatting | bytes 19660800 | tf_op jit(solution)/shard_map/reshape | solution.py:176
  395.7 13.1 %fusion.21 = f32[1920,768]{1,0:T(8,128)} fusion(bf16[1920,2560]{1,0:T(8,128)(2,1)} %reshape.283, bf16[1,2560,768]{2,1,0:T(8,128)(2,1)} %param.21), kind=kOutput, calls=%fused_computation.30 | convolution fusion | flops 7549747200 | bytes 19660800 | tf_op jit(solution)/shard_map/dot_general | solution.py:177
  408.8 27.3 %convolution_convert_fusion = bf16[1920,2560]{1,0:T(8,128)(2,1)} fusion(f32[1920,768]{1,0:T(8,128)} %fusion.21, bf16[1920,2560]{1,0:T(8,128)(2,1)} %reshape.283, bf16[1,768,2560]{2,1,0:T(8,128)(2,1)} %param.23, bf16[1,2560,768]{2,1,0:T(8,128)(2,1)} %param.22), kind=kOutput, calls=%fused_computation.13 | convolution fusion | flops 15113256960 | bytes 33423360 | tf_op jit(solution)/shard_map/dot_general | solution.py:181
  436.1 13.8 %reshape.284 = bf16[128,15,2560]{2,1,0:T(8,128)(2,1)} reshape(bf16[1920,2560]{1,0:T(8,128)(2,1)} %convolution_convert_fusion) | data formatting | bytes 19660800 | tf_op jit(solution)/shard_map/reshape | solution.py:183
  449.9 7.0 %all-to-all-start.5 = ((bf16[128,15,2560]{2,1,0:T(8,128)(2,1)}), bf16[128,15,2560]{2,1,0:T(8,128)(2,1)}, u32[]{:S(2)}, u32[]{:S(2)}) async-start(bf16[128,15,2560]{2,1,0:T(8,128)(2,1)} %reshape.284), calls=%async_computation.5 | async-start | bytes 20971520 | tf_op jit(solution)/shard_map/all_to_all | solution.py:180
  457.5 140.3 %all-to-all-done.5 = bf16[128,15,2560]{2,1,0:T(8,128)(2,1)} async-done(((bf16[128,15,2560]{2,1,0:T(8,128)(2,1)}), bf16[128,15,2560]{2,1,0:T(8,128)(2,1)}, u32[]{:S(2)}, u32[]{:S(2)}) %all-to-all-start.5) | async-done | bytes 9830432 | tf_op jit(solution)/shard_map/all_to_all | solution.py:180
  597.7 11.3 %convert_reduce_fusion = f32[64,15,2560]{2,1,0:T(8,128)} fusion(bf16[128,15,2560]{2,1,0:T(8,128)(2,1)} %all-to-all-done.5), kind=kLoop, calls=%fused_computation.10 | loop fusion | flops 7372800 | bytes 19660800 | tf_op jit(solution)/shard_map/reduce_sum | solution.py:189
  609.1 10.2 %reshape.285 = f32[960,2560]{1,0:T(8,128)} reshape(f32[64,15,2560]{2,1,0:T(8,128)} %convert_reduce_fusion) | data formatting | bytes 19660800 | tf_op jit(solution)/shard_map/reshape | solution.py:191
  619.3 12.2 %gather_fusion = f32[768,2560]{1,0:T(8,128)} fusion(f32[960,2560]{1,0:T(8,128)} %reshape.285, s32[1024]{0:T(1024)S(1)} %pad_clamp_fusion), kind=kCustom, calls=%fused_computation | custom fusion | bytes 15731712 | tf_op jit(solution)/shard_map/gather | solution.py:192
  631.5 9.2 %reshape.286 = f32[128,6,2560]{2,1,0:T(8,128)} reshape(f32[768,2560]{1,0:T(8,128)} %gather_fusion) | data formatting | bytes 15728640 | tf_op jit(solution)/shard_map/reshape | solution.py:192
  640.8 7.9 %multiply_reduce_fusion = f32[128,2560]{1,0:T(8,128)S(1)} fusion(f32[128,6,2560]{2,1,0:T(8,128)} %reshape.286, f32[128,6]{1,0:T(8,128)S(1)} %copy.196), kind=kLoop, calls=%fused_computation.20 | loop fusion | flops 3604480 | bytes 9178112 | tf_op jit(solution)/shard_map/reduce_sum | solution.py:193
  648.7 0.9 fusion.31
  (75 shorter events, 4.1 us)
Async XLA Ops:
  6.5 450.4 %copy-start = (bf16[2560,64]{0,1:T(8,128)(2,1)S(1)}, bf16[2560,64]{0,1:T(8,128)(2,1)}, u32[]{:S(2)}) copy-start(bf16[2560,64]{0,1:T(8,128)(2,1)} %param.19) | copy-start | bytes 983044
  6.5 7.6 %copy-start.9 = (s32[1,4]{1,0:T(1,128)S(1)}, s32[1,4]{1,0:T(1,128)}, u32[]{:S(2)}) copy-start(s32[1,4]{1,0:T(1,128)} %param.15) | copy-start | bytes 52
  6.5 7.9 %copy-start.8 = (s32[1,4,32]{2,1,0:T(4,128)S(1)}, s32[1,4,32]{2,1,0:T(4,128)}, u32[]{:S(2)}) copy-start(s32[1,4,32]{2,1,0:T(4,128)} %param.16) | copy-start | bytes 1540
  6.5 45.9 %copy-start.4 = (bf16[7,128,512]{2,1,0:T(8,128)(2,1)S(1)}, bf16[7,128,512]{2,1,0:T(8,128)(2,1)}, u32[]{:S(2)}) copy-start(bf16[7,128,512]{2,1,0:T(8,128)(2,1)} %param.17) | copy-start | bytes 2752516
  9.7 43.1 %all-to-all-start = ((bf16[8,128,1280]{1,2,0:T(8,128)(2,1)}), bf16[8,128,1280]{1,2,0:T(8,128)(2,1)}, u32[]{:S(2)}, u32[]{:S(2)}) async-start(bf16[8,128,1280]{1,2,0:T(8,128)(2,1)} %stack.2), calls=%async_computation | async-start | bytes 5242880 | tf_op jit(solution)/shard_map/all_to_all | solution.py:78
  84.0 1.8 copy-start.2
  85.8 19.8 %copy-start.6 = (bf16[128,512]{1,0:T(8,128)(2,1)S(1)}, bf16[128,512]{1,0:T(8,128)(2,1)}, u32[]{:S(2)}) copy-start(bf16[128,512]{1,0:T(8,128)(2,1)} %param.14) | copy-start | bytes 393220
  102.2 8.8 %all-to-all-start.3 = ((f32[8,128,2,5]{1,2,3,0:T(2,128)}), f32[8,128,2,5]{1,2,3,0:T(2,128)S(1)}, u32[]{:S(2)}, u32[]{:S(2)}) async-start(f32[8,128,2,5]{1,2,3,0:T(2,128)} %copy.187), calls=%async_computation.3 | async-start | bytes 81920 | tf_op jit(solution)/shard_map/all_to_all | solution.py:112
  105.5 51.4 %all-gather.2.cloned.1.call-start = ((), (), s32[]{:S(2)}) async-start(), calls=%async_computation.6 | async-start | bytes 2228224 | tf_op jit(solution)/shard_map/all_gather | solution.py:132
  110.9 23.7 %all-to-all-start.1 = ((f32[8,128,2,5]{1,2,3,0:T(2,128)}), f32[8,128,2,5]{1,2,3,0:T(2,128)S(1)}, u32[]{:S(2)}, u32[]{:S(2)}) async-start(f32[8,128,2,5]{1,2,3,0:T(2,128)} %copy.167), calls=%async_computation.1 | async-start | bytes 81920 | tf_op jit(solution)/shard_map/all_to_all | solution.py:105
  131.9 7.5 %copy-start.7 = (s32[128,6]{0,1:T(8,128)S(1)}, s32[128,6]{0,1:T(8,128)}, u32[]{:S(2)}) copy-start(s32[128,6]{0,1:T(8,128)} %param.20) | copy-start | bytes 9220
  134.7 65.8 %all-to-all-start.2 = ((f32[8,128,2,5,128]{4,1,3,2,0:T(8,128)}), f32[8,128,2,5,128]{4,1,3,2,0:T(8,128)}, u32[]{:S(2)}, u32[]{:S(2)}) async-start(f32[8,128,2,5,128]{4,1,3,2,0:T(8,128)} %copy.181), calls=%async_computation.2 | async-start | bytes 10485760 | tf_op jit(solution)/shard_map/all_to_all | solution.py:119
  142.8 18.7 %copy-start.3 = (f32[128,2048]{0,1:T(8,128)}, f32[128,2048]{0,1:T(8,128)S(1)}, u32[]{:S(2)}) copy-start(f32[128,2048]{0,1:T(8,128)S(1)} %get-tuple-element.16) | copy-start | bytes 3145732
  161.5 4.0 copy-start.1
  200.4 14.4 %slice-start = ((s8[6553600]{0:T(1024)(128)(4,1)}), s8[2359296]{0:T(1024)(128)(4,1)S(1)}, s32[]{:S(2)}) async-start(s8[6553600]{0:T(1024)(128)(4,1)} %bitcast.137), calls=%async_computation.7 | async-start | bytes 4718592
  206.9 7.9 %slice-start.1 = ((s8[6553600]{0:T(1024)(128)(4,1)}), s8[4194304]{0:T(1024)(128)(4,1)S(1)}, s32[]{:S(2)}) async-start(s8[6553600]{0:T(1024)(128)(4,1)} %bitcast.137), calls=%async_computation.8 | async-start | bytes 8388608
  206.9 7.9 %copy-start.5 = (bf16[128,2560]{1,0:T(8,128)(2,1)S(1)}, bf16[128,2560]{1,0:T(8,128)(2,1)}, u32[]{:S(2)}) copy-start(bf16[128,2560]{1,0:T(8,128)(2,1)} %param.12) | copy-start | bytes 1966084
  449.9 147.8 %all-to-all-start.5 = ((bf16[128,15,2560]{2,1,0:T(8,128)(2,1)}), bf16[128,15,2560]{2,1,0:T(8,128)(2,1)}, u32[]{:S(2)}, u32[]{:S(2)}) async-start(bf16[128,15,2560]{2,1,0:T(8,128)(2,1)} %reshape.284), calls=%async_computation.5 | async-start | bytes 20971520 | tf_op jit(solution)/shard_map/all_to_all | solution.py:180
Sparse Core Ops, SparseCore 0:
  108.5 48.3 all-gather.1
